TPU v7x, 512 devices: a whole 4x8x8 slice. The times are simulated.
512 devices in a mesh: fsdp: 8 (over z_hi, core), seq: 64 (over z_lo, x, y).
Axes of the slice: x: 4, y: 8, z: 8 (z_hi: 4, z_lo: 2; z = z_hi * 2 + z_lo), core: 2. Of those that a mesh axis runs over, the one named last changes fastest.
Arguments:
- hidden: bfloat16 [8192, 8192], P('seq', 'fsdp'), may hold values from -6 to 6
- queries: bfloat16 [8192, 8192], P('seq', 'fsdp'), may hold values from -160 to 160
- kv_weight: bfloat16 [8192, 2048], P('fsdp'), may hold values from -0.09375 to 0.09375
- kv_bias: float32 [2048], replicated, may hold values from -5 to 5
- parents: int32 [64], replicated, may hold values from 0 to 62, as said below
- slot_block: int32 [64], replicated, may hold values from 0 to 63, each once
Outputs:
- attended: bfloat16 [8192, 8192], P('seq', 'fsdp')
Inputs may be any that keep to these rules, and one draw needn't show every extreme that they name: parents[0] = 0; every other block's parent has a lower number; blocks below 32 form one chain from block 0.
All inputs are finite; a program needn't handle non-finite values.
Results may differ from a plain program's by a relative error of at most 0.018.
Values may be sent and summed in bfloat16 or wider, within the bound.
No kernel may reach another device: no remote copies, remote signals or barrier semaphores. Data moves between devices by JAX's collectives and lax.ppermute only.
A program may use at most 64 MiB of HBM per device.

v0:
```python
import math
import jax
import jax.numpy as jnp
from jax import lax
from jax.sharding import PartitionSpec as P

HD = 128
BLOCK = 128


def ancestry_table(parents, slot_block):
    block_count = parents.shape[0]
    block_ids = jnp.arange(block_count, dtype=jnp.int32)
    linked = (parents[:, None] == block_ids[None, :]).astype(jnp.float32)
    ancestry = jnp.maximum(jnp.eye(block_count, dtype=jnp.float32), linked)
    for sweep in range(block_count.bit_length()):
        ancestry = jnp.minimum(jnp.dot(ancestry, ancestry, precision=lax.Precision.HIGHEST), 1.0)
    placement = (slot_block[:, None] == block_ids[None, :]).astype(jnp.float32)
    first_pass = jnp.dot(placement, ancestry, precision=lax.Precision.HIGHEST)
    return jnp.dot(first_pass, placement.T, precision=lax.Precision.HIGHEST)


def keep_state(state_now):
    return state_now


def shards(hidden, queries, kv_weight, kv_bias, parents, slot_block):
    tok_rows = hidden.shape[0]
    per_device = tok_rows // BLOCK
    head_count = queries.shape[1] // HD
    score_scale = 1.0 / math.sqrt(HD)
    fsdp_index = lax.axis_index("fsdp")
    partial_sums = jnp.dot(hidden, kv_weight, preferred_element_type=jnp.float32)
    head_bias = lax.dynamic_slice_in_dim(kv_bias, fsdp_index * 2 * HD, 2 * HD, 0)
    summed = lax.psum(partial_sums, "fsdp")
    head_cols = lax.dynamic_slice_in_dim(summed, fsdp_index * 2 * HD, 2 * HD, 1)
    both_parts = (head_cols + head_bias).astype(jnp.bfloat16)
    key_rows = both_parts[:, :HD]
    value_rows = both_parts[:, HD:]
    visible = ancestry_table(parents, slot_block)
    first_slot = lax.axis_index("seq") * per_device
    own_visible = lax.dynamic_slice_in_dim(visible, first_slot, per_device, 0)
    row_slot = first_slot + jnp.arange(tok_rows, dtype=jnp.int32) // BLOCK
    row_offset = jnp.arange(tok_rows, dtype=jnp.int32) % BLOCK
    query_heads = queries.reshape(tok_rows, head_count, HD)
    initial = (
        jnp.full((tok_rows, head_count), -1e30, jnp.float32),
        jnp.zeros((tok_rows, head_count), jnp.float32),
        jnp.zeros((tok_rows, head_count, HD), jnp.float32),
    )
    key_piece = lax.all_gather(key_rows, "seq", axis=0, tiled=True)
    value_piece = lax.all_gather(value_rows, "seq", axis=0, tiled=True)
    piece_blocks = key_piece.shape[0] // BLOCK
    group = math.gcd(piece_blocks, 8)
    tile = group * BLOCK
    tile_count = piece_blocks // group
    key_offset = jnp.arange(tile, dtype=jnp.int32) % BLOCK
    key_inner = jnp.arange(tile, dtype=jnp.int32) // BLOCK

    def one_tile(tile_index, state_now):
        key_slot_first = tile_index * group
        tile_visible = lax.dynamic_slice_in_dim(own_visible, key_slot_first, group, 1)

        def attend(state_in):
            running_max, running_sum, numerator = state_in
            key_tile = lax.dynamic_slice_in_dim(key_piece, tile_index * tile, tile, 0)
            value_tile = lax.dynamic_slice_in_dim(value_piece, tile_index * tile, tile, 0)
            scores = (
                jnp.einsum("qhd,kd->qhk", query_heads, key_tile, preferred_element_type=jnp.float32)
                * score_scale
            )
            spread = jnp.repeat(jnp.repeat(tile_visible, BLOCK, axis=0), BLOCK, axis=1) > 0.5
            key_slot = key_slot_first + key_inner
            allowed = spread & (
                (row_slot[:, None] != key_slot[None, :])
                | (key_offset[None, :] <= row_offset[:, None])
            )
            masked = jnp.where(allowed[:, None, :], scores, -1e30)
            new_max = jnp.maximum(running_max, jnp.max(masked, axis=-1))
            expo = jnp.where(allowed[:, None, :], jnp.exp(masked - new_max[..., None]), 0.0)
            factor = jnp.exp(running_max - new_max)
            new_sum = running_sum * factor + jnp.sum(expo, axis=-1)
            update = jnp.einsum(
                "qhk,kd->qhd",
                expo.astype(jnp.bfloat16),
                value_tile,
                preferred_element_type=jnp.float32,
            )
            new_numerator = numerator * factor[..., None] + update
            return (new_max, new_sum, new_numerator)

        return lax.cond(jnp.max(tile_visible) > 0.5, attend, keep_state, state_now)

    final_max, final_sum, final_numerator = lax.fori_loop(0, tile_count, one_tile, initial)
    attended = final_numerator / final_sum[..., None]
    return attended.reshape(tok_rows, head_count * HD).astype(jnp.bfloat16)


def solution(mesh):
    return jax.shard_map(
        shards,
        mesh=mesh,
        in_specs=(P("seq", "fsdp"), P("seq", "fsdp"), P("fsdp", None), P(), P(), P()),
        out_specs=P("seq", "fsdp"),
        check_vma=False,
    )
```

profile of v0, /device:TPU:8, one launch (start us, length us, event | category | flops | bytes accessed | tf_op | source)
XLA Modules:
  0.0 772.2 jit_solution(17489612144787789115)
XLA Ops:
  7.5 3.9 fusion.43
  12.2 87.0 %all-reduce.2.cloned.1.call-done = f32[128,2048]{1,0:T(8,128)} async-done(((f32[128,2048]{1,0:T(8,128)}), f32[128,2048]{1,0:T(8,128)}) %all-reduce.2.cloned.1.call-update) | async-done | bytes 1048592 | tf_op jit(solution)/shard_map/psum | solution.py:35
  103.7 297.8 %all-gather.3.cloned.1.call-done = bf16[8192,128]{1,0:T(8,128)(2,1)} async-done(((bf16[128,128]{1,0:T(8,128)(2,1)}), bf16[8192,128]{1,0:T(8,128)(2,1)}) %all-gather.3.cloned.1.call-update) | async-done | bytes 2097168 | tf_op jit(solution)/shard_map/all_gather | solution.py:51
  401.5 301.9 %all-gather.5.cloned.1.call-done = bf16[8192,128]{1,0:T(8,128)(2,1)} async-done(((bf16[128,128]{1,0:T(8,128)(2,1)}), bf16[8192,128]{1,0:T(8,128)(2,1)}) %all-gather.5.cloned.1.call-update) | async-done | bytes 2097168 | tf_op jit(solution)/shard_map/all_gather | solution.py:52
  703.4 61.3 %while.18 = (s32[]{:T(128)}, f32[128,8]{0,1:T(8,128)S(1)}, f32[128,8]{0,1:T(8,128)S(1)}, f32[128,8,128]{2,0,1:T(8,128)S(1)}, f32[1,64]{1,0:T(1,128)S(1)}, /*inde...) while((s32[]{:T(128)}, f32[128,8]{0,1:T(8,128)S(1)}, ...), condition=%wide.region_7.8_spmd.clone, body=%wide.region_1.7_spmd.clone.sunk | while | flops 551307008 | bytes 15081951 | solution.py:94
  704.9 6.2 conditional.3
  705.9 1.7 fusion.8
  707.6 1.0 fusion.10
  708.7 2.4 fusion.14
  712.6 6.2 conditional.3
  713.6 1.7 fusion.8
  715.3 1.0 fusion.10
  716.3 2.4 fusion.14
  720.2 6.2 conditional.3
  721.2 1.7 fusion.8
  723.0 1.0 fusion.10
  724.0 2.4 fusion.14
  727.9 6.2 conditional.3
  728.9 1.7 fusion.8
  731.7 2.4 fusion.14
  735.6 6.2 conditional.3
  736.6 1.7 fusion.8
  739.3 2.4 fusion.14
  743.2 6.2 conditional.3
  744.2 1.7 fusion.8
  747.0 2.4 fusion.14
  750.9 6.2 conditional.3
  751.9 1.7 fusion.8
  754.7 2.4 fusion.14
  758.6 6.2 conditional.3
  759.6 1.7 fusion.8
  762.3 2.4 fusion.14
  (174 shorter events, 25.9 us)
Async XLA Ops:
  6.5 1.0 copy-start
  6.5 95.0 %copy-start.1 = (bf16[128,1024]{1,0:T(8,128)(2,1)S(1)}, bf16[128,1024]{1,0:T(8,128)(2,1)}, u32[]{:S(2)}) copy-start(bf16[128,1024]{1,0:T(8,128)(2,1)} %param.11) | copy-start | bytes 786436
  6.5 95.4 %copy-start.3 = (s32[64]{0:T(128)S(1)}, s32[64]{0:T(128)}, u32[]{:S(2)}) copy-start(s32[64]{0:T(128)} %param.14) | copy-start | bytes 772
  6.5 96.6 %copy-start.2 = (s32[64]{0:T(128)S(1)}, s32[64]{0:T(128)}, u32[]{:S(2)}) copy-start(s32[64]{0:T(128)} %param.15) | copy-start | bytes 772
  6.5 92.7 %all-reduce.2.cloned.1.call-start = ((), (), s32[]{:S(2)}) async-start(), calls=%async_computation | async-start | bytes 2097152 | tf_op jit(solution)/shard_map/psum | solution.py:35
  11.4 390.1 %all-gather.3.cloned.1.call-start = ((), (), s32[]{:S(2)}) async-start(), calls=%async_computation.1 | async-start | bytes 2129920 | tf_op jit(solution)/shard_map/all_gather | solution.py:51
  100.8 602.6 %all-gather.5.cloned.1.call-start = ((), (), s32[]{:S(2)}) async-start(), calls=%async_computation.2 | async-start | bytes 2129920 | tf_op jit(solution)/shard_map/all_gather | solution.py:52
Sparse Core Ops, SparseCore 0:
  11.5 87.6 all-reduce.1
  101.3 300.1 all-gather.2
  403.6 299.7 all-gather.4
where the time goes:
time: 773 us; the launch traced here: 772 us
  waiting for transfers between devices  687 us (89%)
  matrix products  38.3 us (5%)
  other arithmetic  23 us (3%)
  between operations  13.3 us (2%)
    all_gather x1, waiting for transfers between devices, shards(): value_piece = lax.all_gather(value_rows, 'seq', axis=0, tiled=True)  302 us
    all_gather x1, waiting for transfers between devices, shards(): key_piece = lax.all_gather(key_rows, 'seq', axis=0, tiled=True)  298 us
    psum x1, waiting for transfers between devices, shards(): summed = lax.psum(partial_sums, 'fsdp')  87 us
    dot_general x8, matrix products, attend(): jnp.einsum('qhk,kd->qhd', expo.astype(jnp.bfloat16), value_tile, preferre...  19.1 us
  transfers between devices with their start and end apart: 3, of which 3 were waited for; matrix products, arithmetic and copies ran while one was open for 0% of the time, Pallas kernels for 0%

commit v1 on v0

--- a/solution.py
+++ b/solution.py
@@ -6,6 +6,14 @@
 
 HD = 128
 BLOCK = 128
+
+
+def time_the_record(in_array, at_axis):
+    block_last = lax.axis_size("seq")
+    f_next = jnp.stack([in_array] * block_last)
+    built = lax.all_to_all(f_next, concat_axis=0, axis_name="seq", split_axis=0)
+    z2 = jnp.concatenate(built, axis=at_axis)
+    return z2
 
 
 def ancestry_table(parents, slot_block):
@@ -49,7 +57,7 @@
         jnp.zeros((tok_rows, head_count, HD), jnp.float32),
     )
     key_piece = lax.all_gather(key_rows, "seq", axis=0, tiled=True)
-    value_piece = lax.all_gather(value_rows, "seq", axis=0, tiled=True)
+    value_piece = time_the_record(value_rows, 0)
     piece_blocks = key_piece.shape[0] // BLOCK
     group = math.gcd(piece_blocks, 8)
     tile = group * BLOCK

time: 773 us -> 478 us (0.62)
  waiting for transfers between devices: 687 us -> 390 us
  starting transfers between devices: 0.12 us -> 10.6 us
    all_gather x1 -> x0, waiting for transfers between devices: 302 us -> none  [shards(): value_piece = lax.all_gather(value_rows, 'seq', axis=0, tiled=True)]
    all_to_all x0 -> x1, waiting for transfers between devices: none -> 51.2 us  [time_the_record(): built = lax.all_to_all(f_next, concat_axis=0, axis_name='seq', split_axis=0)]
    all_gather x1, waiting for transfers between devices: 298 us -> 251 us  [shards(): key_piece = lax.all_gather(key_rows, 'seq', axis=0, tiled=True)]
    all_to_all x0 -> x1, starting transfers between devices: none -> 10.5 us  [time_the_record(): built = lax.all_to_all(f_next, concat_axis=0, axis_name='seq', split_axis=0)]
  transfers between devices with their start and end apart: 3 -> 3, of which waited for: 3 -> 3; matrix products, arithmetic and copies ran while one was open for 0% -> 1% of each run, Pallas kernels for 0% -> 0%
where the time goes in v1:
time: 478 us
  waiting for transfers between devices  390 us (82%)
  matrix products  30.6 us (6%)
  other arithmetic  22.3 us (5%)
  between operations  13.6 us (3%)
  starting transfers between devices  10.6 us (2%)
  loops' own time  5.63 us (1%)
  local copies, waits for them, and re-layouts  5.29 us (1%)
    all_gather x1, waiting for transfers between devices, shards(): key_piece = lax.all_gather(key_rows, 'seq', axis=0, tiled=True)  251 us
    psum x1, waiting for transfers between devices, shards(): summed = lax.psum(partial_sums, 'fsdp')  87 us
    all_to_all x1, waiting for transfers between devices, time_the_record(): built = lax.all_to_all(f_next, concat_axis=0, axis_name='seq', split_axis=0)  51.2 us
    dot_general x8, matrix products, attend(): jnp.einsum('qhd,kd->qhk', query_heads, key_tile, preferred_element_type=j...  13.7 us
    dot_general x8, matrix products, attend(): jnp.einsum('qhk,kd->qhd', expo.astype(jnp.bfloat16), value_tile, preferre...  11.4 us
    all_to_all x1, starting transfers between devices, time_the_record(): built = lax.all_to_all(f_next, concat_axis=0, axis_name='seq', split_axis=0)  10.5 us
  transfers between devices with their start and end apart: 3, of which 3 were waited for; matrix products, arithmetic and copies ran while one was open for 1% of the time, Pallas kernels for 0%

profile of v1, /device:TPU:8, one launch (start us, length us, event | category | flops | bytes accessed | tf_op | source)
XLA Modules:
  0.0 477.5 jit_solution(13947221437388648741)
XLA Ops:
  7.5 3.9 fusion.43
  12.2 87.0 %all-reduce.2.cloned.1.call-done = f32[128,2048]{1,0:T(8,128)} async-done(((f32[128,2048]{1,0:T(8,128)}), f32[128,2048]{1,0:T(8,128)}) %all-reduce.2.cloned.1.call-update) | async-done | bytes 1048592 | tf_op jit(solution)/shard_map/psum | solution.py:43
  100.8 1.8 stack.2
  102.6 10.5 %all-to-all-start = ((bf16[64,128,128]{2,1,0:T(8,128)(2,1)}), bf16[64,128,128]{2,1,0:T(8,128)(2,1)S(1)}, u32[]{:S(2)}, u32[]{:S(2)}) async-start(bf16[64,128,128]{2,1,0:T(8,128)(2,1)} %stack.2), calls=%async_computation | async-start | bytes 4194304 | tf_op jit(solution)/shard_map/all_to_all | solution.py:14
  116.0 51.2 %all-to-all-done = bf16[64,128,128]{2,1,0:T(8,128)(2,1)S(1)} async-done(((bf16[64,128,128]{2,1,0:T(8,128)(2,1)}), bf16[64,128,128]{2,1,0:T(8,128)(2,1)S(1)}, u32[]{:S(2)}, u32[]{:S(2)}) %all-to-all-start) | async-done | bytes 2097184 | tf_op jit(solution)/shard_map/all_to_all | solution.py:14
  167.3 250.7 %all-gather.2.cloned.1.call-done = bf16[8192,128]{1,0:T(8,128)(2,1)} async-done(((bf16[128,128]{1,0:T(8,128)(2,1)}), bf16[8192,128]{1,0:T(8,128)(2,1)}) %all-gather.2.cloned.1.call-update) | async-done | bytes 2097168 | tf_op jit(solution)/shard_map/all_gather | solution.py:59
  418.0 51.8 %while.18 = (s32[]{:T(128)}, f32[128,8]{0,1:T(8,128)S(1)}, f32[128,8]{0,1:T(8,128)S(1)}, f32[128,8,128]{2,0,1:T(8,128)S(1)}, f32[1,64]{1,0:T(1,128)S(1)}, /*inde...) while((s32[]{:T(128)}, f32[128,8]{0,1:T(8,128)S(1)}, ...), condition=%wide.region_7.8_spmd.clone, body=%wide.region_1.7_spmd.clone.sunk | while | flops 551307008 | bytes 15081951 | solution.py:102
  419.2 5.2 %conditional.3 = ((f32[128,8]{0,1:T(8,128)S(1)}, f32[128,8]{0,1:T(8,128)S(1)}, f32[128,8,128]{2,0,1:T(8,128)S(1)})) conditional(s32[]{:T(128)} %convert_element_type.51, (f32[128,8]{0,1:T(8,128)S(1)}, f32[128,8]{0,1:T(8,128)S(1)}, f32[128,8,128]{2,0,1:T(8,128)S(1)}) %tuple.59, (f32[1,8]{1,0:T(1,128)S(1)}, s32[]{:T(128)}, s32[]{:T(128)}, ...), branch_computations={%region_3.3_spmd, %region_4.6_spmd.clone} | conditional | flops 551302400 | bytes 15061798 | solution.py:100
  420.2 1.7 fusion.8
  422.0 1.0 fusion.10
  423.0 1.4 fusion.14
  425.7 5.2 %conditional.3 = ((f32[128,8]{0,1:T(8,128)S(1)}, f32[128,8]{0,1:T(8,128)S(1)}, f32[128,8,128]{2,0,1:T(8,128)S(1)})) conditional(s32[]{:T(128)} %convert_element_type.51, (f32[128,8]{0,1:T(8,128)S(1)}, f32[128,8]{0,1:T(8,128)S(1)}, f32[128,8,128]{2,0,1:T(8,128)S(1)}) %tuple.59, (f32[1,8]{1,0:T(1,128)S(1)}, s32[]{:T(128)}, s32[]{:T(128)}, ...), branch_computations={%region_3.3_spmd, %region_4.6_spmd.clone} | conditional | flops 551302400 | bytes 15061798 | solution.py:100
  426.7 1.7 fusion.8
  429.5 1.4 fusion.14
  432.2 5.2 %conditional.3 = ((f32[128,8]{0,1:T(8,128)S(1)}, f32[128,8]{0,1:T(8,128)S(1)}, f32[128,8,128]{2,0,1:T(8,128)S(1)})) conditional(s32[]{:T(128)} %convert_element_type.51, (f32[128,8]{0,1:T(8,128)S(1)}, f32[128,8]{0,1:T(8,128)S(1)}, f32[128,8,128]{2,0,1:T(8,128)S(1)}) %tuple.59, (f32[1,8]{1,0:T(1,128)S(1)}, s32[]{:T(128)}, s32[]{:T(128)}, ...), branch_computations={%region_3.3_spmd, %region_4.6_spmd.clone} | conditional | flops 551302400 | bytes 15061798 | solution.py:100
  433.2 1.7 fusion.8
  435.9 1.4 fusion.14
  438.7 5.2 %conditional.3 = ((f32[128,8]{0,1:T(8,128)S(1)}, f32[128,8]{0,1:T(8,128)S(1)}, f32[128,8,128]{2,0,1:T(8,128)S(1)})) conditional(s32[]{:T(128)} %convert_element_type.51, (f32[128,8]{0,1:T(8,128)S(1)}, f32[128,8]{0,1:T(8,128)S(1)}, f32[128,8,128]{2,0,1:T(8,128)S(1)}) %tuple.59, (f32[1,8]{1,0:T(1,128)S(1)}, s32[]{:T(128)}, s32[]{:T(128)}, ...), branch_computations={%region_3.3_spmd, %region_4.6_spmd.clone} | conditional | flops 551302400 | bytes 15061798 | solution.py:100
  439.7 1.7 fusion.8
  442.4 1.4 fusion.14
  445.1 5.2 %conditional.3 = ((f32[128,8]{0,1:T(8,128)S(1)}, f32[128,8]{0,1:T(8,128)S(1)}, f32[128,8,128]{2,0,1:T(8,128)S(1)})) conditional(s32[]{:T(128)} %convert_element_type.51, (f32[128,8]{0,1:T(8,128)S(1)}, f32[128,8]{0,1:T(8,128)S(1)}, f32[128,8,128]{2,0,1:T(8,128)S(1)}) %tuple.59, (f32[1,8]{1,0:T(1,128)S(1)}, s32[]{:T(128)}, s32[]{:T(128)}, ...), branch_computations={%region_3.3_spmd, %region_4.6_spmd.clone} | conditional | flops 551302400 | bytes 15061798 | solution.py:100
  446.1 1.7 fusion.8
  448.9 1.4 fusion.14
  451.6 5.2 %conditional.3 = ((f32[128,8]{0,1:T(8,128)S(1)}, f32[128,8]{0,1:T(8,128)S(1)}, f32[128,8,128]{2,0,1:T(8,128)S(1)})) conditional(s32[]{:T(128)} %convert_element_type.51, (f32[128,8]{0,1:T(8,128)S(1)}, f32[128,8]{0,1:T(8,128)S(1)}, f32[128,8,128]{2,0,1:T(8,128)S(1)}) %tuple.59, (f32[1,8]{1,0:T(1,128)S(1)}, s32[]{:T(128)}, s32[]{:T(128)}, ...), branch_computations={%region_3.3_spmd, %region_4.6_spmd.clone} | conditional | flops 551302400 | bytes 15061798 | solution.py:100
  452.6 1.7 fusion.8
  455.4 1.4 fusion.14
  458.1 5.2 %conditional.3 = ((f32[128,8]{0,1:T(8,128)S(1)}, f32[128,8]{0,1:T(8,128)S(1)}, f32[128,8,128]{2,0,1:T(8,128)S(1)})) conditional(s32[]{:T(128)} %convert_element_type.51, (f32[128,8]{0,1:T(8,128)S(1)}, f32[128,8]{0,1:T(8,128)S(1)}, f32[128,8,128]{2,0,1:T(8,128)S(1)}) %tuple.59, (f32[1,8]{1,0:T(1,128)S(1)}, s32[]{:T(128)}, s32[]{:T(128)}, ...), branch_computations={%region_3.3_spmd, %region_4.6_spmd.clone} | conditional | flops 551302400 | bytes 15061798 | solution.py:100
  459.1 1.7 fusion.8
  461.9 1.4 fusion.14
  464.6 5.2 %conditional.3 = ((f32[128,8]{0,1:T(8,128)S(1)}, f32[128,8]{0,1:T(8,128)S(1)}, f32[128,8,128]{2,0,1:T(8,128)S(1)})) conditional(s32[]{:T(128)} %convert_element_type.51, (f32[128,8]{0,1:T(8,128)S(1)}, f32[128,8]{0,1:T(8,128)S(1)}, f32[128,8,128]{2,0,1:T(8,128)S(1)}) %tuple.59, (f32[1,8]{1,0:T(1,128)S(1)}, s32[]{:T(128)}, s32[]{:T(128)}, ...), branch_computations={%region_3.3_spmd, %region_4.6_spmd.clone} | conditional | flops 551302400 | bytes 15061798 | solution.py:100
  465.6 1.7 fusion.8
  468.3 1.4 fusion.14
  (174 shorter events, 27.1 us)
Async XLA Ops:
  6.5 1.0 copy-start
  6.5 92.7 %all-reduce.2.cloned.1.call-start = ((), (), s32[]{:S(2)}) async-start(), calls=%async_computation.1 | async-start | bytes 2097152 | tf_op jit(solution)/shard_map/psum | solution.py:43
  11.4 102.5 %copy-start.1 = (bf16[128,1024]{1,0:T(8,128)(2,1)S(1)}, bf16[128,1024]{1,0:T(8,128)(2,1)}, u32[]{:S(2)}) copy-start(bf16[128,1024]{1,0:T(8,128)(2,1)} %param.11) | copy-start | bytes 786436
  11.4 102.9 %copy-start.3 = (s32[64]{0:T(128)S(1)}, s32[64]{0:T(128)}, u32[]{:S(2)}) copy-start(s32[64]{0:T(128)} %param.14) | copy-start | bytes 772
  12.2 103.3 %copy-start.2 = (s32[64]{0:T(128)S(1)}, s32[64]{0:T(128)}, u32[]{:S(2)}) copy-start(s32[64]{0:T(128)} %param.15) | copy-start | bytes 772
  102.6 64.7 %all-to-all-start = ((bf16[64,128,128]{2,1,0:T(8,128)(2,1)}), bf16[64,128,128]{2,1,0:T(8,128)(2,1)S(1)}, u32[]{:S(2)}, u32[]{:S(2)}) async-start(bf16[64,128,128]{2,1,0:T(8,128)(2,1)} %stack.2), calls=%async_computation | async-start | bytes 4194304 | tf_op jit(solution)/shard_map/all_to_all | solution.py:14
  113.2 304.8 %all-gather.2.cloned.1.call-start = ((), (), s32[]{:S(2)}) async-start(), calls=%async_computation.2 | async-start | bytes 2129920 | tf_op jit(solution)/shard_map/all_gather | solution.py:59
Sparse Core Ops, SparseCore 0:
  11.5 87.6 all-reduce.1
  116.1 301.8 all-gather.1
